TPU v7x, 256 devices: a whole 4x4x8 slice. The times are simulated.
256 devices in a mesh: space: 32 (over y_lo, z, core), chan: 8 (over x, y_hi).
Axes of the slice: x: 4, y: 4 (y_hi: 2, y_lo: 2; y = y_hi * 2 + y_lo), z: 8, core: 2. Of those that a mesh axis runs over, the one named last changes fastest.
Arguments:
- inputs: bfloat16 [32, 256, 2048], P('space', 'chan'), may hold values from -6 to 6
- weights: bfloat16 [27, 256, 256], P(None, 'chan'), may hold values from -0.078125 to 0.078125
- cotangent: bfloat16 [32, 256, 2048], P('space', 'chan'), may hold values from -6 to 6
Outputs:
- output: bfloat16 [32, 256, 2048], P('space', 'chan')
- input_grad: bfloat16 [32, 256, 2048], P('space', 'chan')
- weight_grad: float32 [27, 256, 256], P(None, 'chan')
All inputs are finite; a program needn't handle non-finite values.
Results may differ from a plain program's by a relative error of at most 0.001.
Values may be sent and summed in bfloat16 or wider, within the bound.
No kernel may reach another device: no remote copies, remote signals or barrier semaphores. Data moves between devices by JAX's collectives and lax.ppermute only.
A program may use at most 192 MiB of HBM per device.

v0:
```python
import jax
import jax.numpy as jnp
from jax import lax
from jax.sharding import PartitionSpec as P

PLANE_ROWS = 32
ROW_CELLS = 64


def extended(block, sides, width):
    for axis, dim in sides:
        count = lax.axis_size(axis)
        forward = [(i, i + 1) for i in range(count - 1)]
        backward = [(target, source) for source, target in forward]
        low = lax.ppermute(
            lax.slice_in_dim(block, block.shape[dim] - width, None, axis=dim), axis, forward
        )
        high = lax.ppermute(lax.slice_in_dim(block, 0, width, axis=dim), axis, backward)
        block = jnp.concatenate([low, block, high], axis=dim)
    return block


def plane_shift(field, tap_row, tap_col):
    lead = field.shape[:-1]
    grid = field.reshape(lead + (PLANE_ROWS, ROW_CELLS))
    padded = jnp.pad(grid, [(0, 0)] * len(lead) + [(1, 1), (1, 1)])
    window = padded[..., tap_row : tap_row + PLANE_ROWS, tap_col : tap_col + ROW_CELLS]
    return window.reshape(lead + (PLANE_ROWS * ROW_CELLS,))


def stack_at(padded, tap_row, tap_col):
    planes = padded.shape[0] - 2
    moved = plane_shift(padded, tap_row, tap_col)
    return jnp.concatenate(
        [moved[tap_depth : tap_depth + planes] for tap_depth in range(3)], axis=1
    )


def tap_weights(taps, tap_row, tap_col):
    return jnp.concatenate(
        [taps[tap_depth * 9 + tap_row * 3 + tap_col] for tap_depth in range(3)], axis=0
    )


def convolve(padded, taps):
    total = None
    for tap_row in range(3):
        for tap_col in range(3):
            term = jnp.einsum(
                "dcp,co->dop",
                stack_at(padded, tap_row, tap_col),
                tap_weights(taps, tap_row, tap_col),
                preferred_element_type=jnp.float32,
            )
            total = term if total is None else total + term
    return total


def weight_terms(padded, cot_whole, channels):
    pieces = [None] * 27
    for tap_row in range(3):
        for tap_col in range(3):
            block = jnp.einsum(
                "dcp,dop->co",
                stack_at(padded, tap_row, tap_col),
                cot_whole,
                preferred_element_type=jnp.float32,
            )
            block = block.reshape(3, channels, cot_whole.shape[1])
            for tap_depth in range(3):
                pieces[tap_depth * 9 + tap_row * 3 + tap_col] = block[tap_depth]
    return jnp.stack(pieces, axis=0)


def local(inputs, weights, cotangent):
    padded = extended(inputs, (("space", 0),), 1)
    partial_out = convolve(padded, weights)
    output = lax.psum_scatter(partial_out, "chan", scatter_dimension=1, tiled=True).astype(
        jnp.bfloat16
    )
    gathered = lax.all_gather(cotangent, "chan", axis=1, tiled=True)
    cot_padded = extended(gathered, (("space", 0),), 1)
    cot_whole = cot_padded[1:-1]
    flipped = jnp.transpose(weights[::-1], (0, 2, 1))
    input_grad = convolve(cot_padded, flipped).astype(jnp.bfloat16)
    local_terms = weight_terms(padded, cot_whole, inputs.shape[1])
    weight_grad = lax.psum(local_terms, "space")
    return (output, input_grad, weight_grad)


def solution(mesh):
    placed = (P("space", "chan", None), P(None, "chan", None), P("space", "chan", None))
    return jax.shard_map(
        local,
        mesh=mesh,
        in_specs=placed,
        out_specs=(P("space", "chan", None), P("space", "chan", None), P(None, "chan", None)),
        check_vma=False,
    )
```

profile of v0, /device:TPU:24, one launch (start us, length us, event | category | flops | bytes accessed | tf_op | source)
XLA Modules:
  0.0 384.9 jit_solution(320602423577932100)
XLA Ops:
  7.2 7.4 %collective-permute-start.1 = (bf16[1,32,2048]{2,1,0:T(8,128)(2,1)}, bf16[1,32,2048]{2,1,0:T(8,128)(2,1)S(1)}, u32[]{:S(2)}, u32[]{:S(2)}) collective-permute-start(bf16[1,32,2048]{2,1,0:T(8,128)(2,1)} %param.3), channel_id=1, source_target_pairs={{8,0},{16,8},{24,16},{32,24},{40,32},{48,40},{56,48},{64,56},{72,6... | collective-permute-start | bytes 393224 | tf_op jit(solution)/shard_map/ppermute | solution.py:18
  14.6 1.9 collective-permute-start
  16.6 1.5 slice_bitcast_fusion.54
  18.1 1.7 slice_bitcast_fusion.56
  19.8 1.0 reverse_bitcast_fusion
  20.8 0.8 slice_bitcast_fusion.29
  21.6 0.7 slice_bitcast_fusion.47
  22.3 0.9 collective-permute-done
  23.2 0.7 copy-done.58
  23.9 0.9 pad_maximum_fusion.1
  24.8 0.8 reshape.279
  25.6 1.5 pad_slice_fusion.25
  27.1 2.8 pad_slice_fusion.26
  29.9 1.3 slice.794
  31.2 1.9 slice.785
  33.1 1.9 slice.787
  35.0 1.9 slice.796
  36.9 1.9 slice.726
  38.8 1.9 slice.792
  40.7 1.9 slice.728
  42.5 1.9 slice.730
  44.4 1.9 slice.735
  46.3 1.9 slice.737
  48.2 1.9 slice.739
  50.0 0.9 slice.744
  51.0 0.9 slice.746
  51.9 0.9 slice.748
  52.8 0.9 slice.753
  53.8 0.9 slice.755
  57.5 1.5 fusion.76
  62.7 0.7 convolution_add_fusion.1
  63.5 1.8 fusion.45
  65.3 1.3 all-gather.2.cloned.1.call-done
  66.6 1.6 copy.7
  68.2 4.3 %collective-permute-start.3 = (bf16[1,256,2048]{1,2,0:T(8,128)(2,1)S(1)}, bf16[1,256,2048]{1,2,0:T(8,128)(2,1)S(1)}, u32[]{:S(2)}, u32[]{:S(2)}) collective-permute-start(bf16[1,256,2048]{1,2,0:T(8,128)(2,1)S(1)} %copy.7), channel_id=1, source_target_pairs={{8,0},{16,8},{24,16},{32,24},{40,32},{48,40},{56,48},{64,56},{72,6... | collective-permute-start | bytes 3145736 | tf_op jit(solution)/shard_map/ppermute | solution.py:18
  72.5 1.9 collective-permute-start.2
  74.4 1.9 fusion.73
  76.4 0.6 constant_dynamic-update-slice_fusion.26
  77.0 1.5 fusion.71
  78.5 0.6 constant_dynamic-update-slice_fusion.25
  79.1 1.5 fusion.69
  80.6 0.6 constant_dynamic-update-slice_fusion.24
  81.8 0.6 constant_dynamic-update-slice_fusion.23
  82.9 0.6 constant_dynamic-update-slice_fusion.22
  84.0 0.6 constant_dynamic-update-slice_fusion.21
  85.1 0.6 constant_dynamic-update-slice_fusion.20
  86.2 0.6 constant_dynamic-update-slice_fusion.19
  87.2 0.6 constant_dynamic-update-slice_fusion.18
  99.0 1.9 pad_maximum_fusion
  101.0 3.5 pad_slice_fusion.1
  104.5 8.9 %pad_slice_fusion.2 = (bf16[1,256,32,64]{1,3,2,0:T(8,128)(2,1)S(1)}, bf16[1,256,32,64]{1,3,2,0:T(8,128)(2,1)}, bf16[1,256,32,64]{1,3,2,0:T(8,128)(2,1)}, bf16[1,...) fusion(bf16[3,256,32,64]{1,3,2,0:T(8,128)(2,1)S(1)} %bitcast.398), kind=kLoop, calls=%fused_computation.94 | loop fusion | bytes 23068672 | tf_op jit(solution)/shard_map/slice | solution.py:35
  113.5 3.0 fusion
  116.7 1.0 fusion.25
  118.6 1.0 fusion.54
  120.4 1.0 fusion.53
  121.5 1.0 fusion.52
  122.7 2.3 fusion.51
  125.1 1.0 fusion.49
  126.6 1.0 fusion.48
  128.1 1.7 fusion.56
  129.8 22.9 %reduce-scatter.2.cloned.1.call-done = f32[1,32,2048]{2,1,0:T(8,128)} async-done(((f32[1,256,2048]{2,1,0:T(8,128)}), f32[1,32,2048]{2,1,0:T(8,128)}) %reduce-scatter.2.cloned.1.call-update) | async-done | bytes 262160 | tf_op jit(solution)/shard_map/reduce_scatter | solution.py:78
  152.7 1.6 convert_element_type.38
  154.4 221.8 %all-reduce.4.cloned.1.call-done = f32[27,32,256]{2,1,0:T(8,128)} async-done(((f32[27,32,256]{2,1,0:T(8,128)}), f32[27,32,256]{2,1,0:T(8,128)}) %all-reduce.4.cloned.1.call-update) | async-done | bytes 884752 | tf_op jit(solution)/shard_map/psum | solution.py:87
  376.2 2.2 copy.38
  (268 shorter events, 23.1 us)
Async XLA Ops:
  7.2 59.4 %all-gather.2.cloned.1.call-start = ((), (), s32[]{:S(2)}) async-start(), calls=%async_computation.2 | async-start | bytes 1179648 | tf_op jit(solution)/shard_map/all_gather | solution.py:81
  7.2 15.0 %collective-permute-start.1 = (bf16[1,32,2048]{2,1,0:T(8,128)(2,1)}, bf16[1,32,2048]{2,1,0:T(8,128)(2,1)S(1)}, u32[]{:S(2)}, u32[]{:S(2)}) collective-permute-start(bf16[1,32,2048]{2,1,0:T(8,128)(2,1)} %param.3), channel_id=1, source_target_pairs={{8,0},{16,8},{24,16},{32,24},{40,32},{48,40},{56,48},{64,56},{72,6... | collective-permute-start | bytes 393224 | tf_op jit(solution)/shard_map/ppermute | solution.py:18
  14.6 8.6 %collective-permute-start = (bf16[1,32,2048]{2,1,0:T(8,128)(2,1)}, bf16[1,32,2048]{2,1,0:T(8,128)(2,1)S(1)}, u32[]{:S(2)}, u32[]{:S(2)}) collective-permute-start(bf16[1,32,2048]{2,1,0:T(8,128)(2,1)} %param.3), channel_id=1, source_target_pairs={{0,8},{8,16},{16,24},{24,32},{32,40},{40,48},{48,56},{56,64},{64,7... | collective-permute-start | bytes 393224 | tf_op jit(solution)/shard_map/ppermute | solution.py:15
  16.6 136.2 %reduce-scatter.2.cloned.1.call-start = ((), (), s32[]{:S(2)}) async-start(), calls=%async_computation.1 | async-start | bytes 2359296 | tf_op jit(solution)/shard_map/reduce_scatter | solution.py:78
  29.9 20.1 %copy-start.11 = (bf16[1,32,32,64]{3,2,1,0:T(8,128)(2,1)S(1)}, bf16[1,32,32,64]{3,2,1,0:T(8,128)(2,1)}, u32[]{:S(2)}) copy-start(bf16[1,32,32,64]{3,2,1,0:T(8,128)(2,1)} %get-tuple-element.33) | copy-start | bytes 393220
  29.9 21.0 %copy-start.10 = (bf16[1,32,32,64]{3,2,1,0:T(8,128)(2,1)S(1)}, bf16[1,32,32,64]{3,2,1,0:T(8,128)(2,1)}, u32[]{:S(2)}) copy-start(bf16[1,32,32,64]{3,2,1,0:T(8,128)(2,1)} %get-tuple-element.34) | copy-start | bytes 393220
  29.9 22.0 %copy-start.9 = (bf16[1,32,32,64]{3,2,1,0:T(8,128)(2,1)S(1)}, bf16[1,32,32,64]{3,2,1,0:T(8,128)(2,1)}, u32[]{:S(2)}) copy-start(bf16[1,32,32,64]{3,2,1,0:T(8,128)(2,1)} %get-tuple-element.35) | copy-start | bytes 393220
  53.8 3.7 copy-start.35
  53.8 3.7 copy-start.40
  54.7 2.3 copy-start.81
  54.7 2.3 copy-start.82
  54.7 2.3 copy-start.83
  55.0 5.3 %copy-start.51 = (bf16[1,32,2048]{2,1,0:T(8,128)(2,1)}, bf16[1,32,2048]{2,1,0:T(8,128)(2,1)S(1)}, u32[]{:S(2)}) copy-start(bf16[1,32,2048]{2,1,0:T(8,128)(2,1)S(1)} %slice.757) | copy-start | bytes 393220
  55.2 3.8 copy-start.27
  55.5 3.5 copy-start.31
  55.8 3.3 copy-start.36
  56.1 5.7 %copy-start.29 = (bf16[1,32,2048]{2,1,0:T(8,128)(2,1)}, bf16[1,32,2048]{2,1,0:T(8,128)(2,1)S(1)}, u32[]{:S(2)}) copy-start(bf16[1,32,2048]{2,1,0:T(8,128)(2,1)S(1)} %slice.774) | copy-start | bytes 393220
  56.1 3.0 copy-start.41
  56.1 3.0 copy-start.45
  56.1 3.0 copy-start.49
  56.1 3.0 copy-start.73
  56.1 3.0 copy-start.74
  56.1 3.0 copy-start.75
  56.4 5.4 %copy-start.33 = (bf16[1,32,2048]{2,1,0:T(8,128)(2,1)}, bf16[1,32,2048]{2,1,0:T(8,128)(2,1)S(1)}, u32[]{:S(2)}) copy-start(bf16[1,32,2048]{2,1,0:T(8,128)(2,1)S(1)} %slice.776) | copy-start | bytes 393220
  56.7 5.1 %copy-start.38 = (bf16[1,32,2048]{2,1,0:T(8,128)(2,1)}, bf16[1,32,2048]{2,1,0:T(8,128)(2,1)S(1)}, u32[]{:S(2)}) copy-start(bf16[1,32,2048]{2,1,0:T(8,128)(2,1)S(1)} %slice.778) | copy-start | bytes 393220
  57.0 5.5 %copy-start.25 = (bf16[1,32,2048]{2,1,0:T(8,128)(2,1)}, bf16[1,32,2048]{2,1,0:T(8,128)(2,1)S(1)}, u32[]{:S(2)}) copy-start(bf16[1,32,2048]{2,1,0:T(8,128)(2,1)S(1)} %slice.783) | copy-start | bytes 393220
  57.5 2.2 copy-start.42
  57.5 2.2 copy-start.46
  57.5 2.2 copy-start.50
  57.5 2.2 copy-start.69
  57.5 2.2 copy-start.79
  57.5 2.2 copy-start.80
  65.2 310.9 %all-reduce.4.cloned.1.call-start = ((), (), s32[]{:S(2)}) async-start(), calls=%async_computation.3 | async-start | bytes 1769472 | tf_op jit(solution)/shard_map/psum | solution.py:87
  66.6 10.4 %copy-start.12 = (bf16[1,256,2048]{2,1,0:T(8,128)(2,1)S(1)}, bf16[1,256,2048]{2,1,0:T(8,128)(2,1)}, u32[]{:S(2)}) copy-start(bf16[1,256,2048]{2,1,0:T(8,128)(2,1)} %all-gather.2.cloned.1.call-done) | copy-start | bytes 3145732
  68.1 13.1 %copy-start.44 = (bf16[1,32,2048]{2,1,0:T(8,128)(2,1)S(1)}, bf16[1,32,2048]{2,1,0:T(8,128)(2,1)}, u32[]{:S(2)}) copy-start(bf16[1,32,2048]{2,1,0:T(8,128)(2,1)} %slice.753) | copy-start | bytes 393220
  68.2 13.1 %copy-start.48 = (bf16[1,32,2048]{2,1,0:T(8,128)(2,1)S(1)}, bf16[1,32,2048]{2,1,0:T(8,128)(2,1)}, u32[]{:S(2)}) copy-start(bf16[1,32,2048]{2,1,0:T(8,128)(2,1)} %slice.755) | copy-start | bytes 393220
  68.2 13.1 %copy-start.52 = (bf16[1,32,2048]{2,1,0:T(8,128)(2,1)S(1)}, bf16[1,32,2048]{2,1,0:T(8,128)(2,1)}, u32[]{:S(2)}) copy-start(bf16[1,32,2048]{2,1,0:T(8,128)(2,1)} %copy-done.51) | copy-start | bytes 393220
  68.2 30.8 %collective-permute-start.3 = (bf16[1,256,2048]{1,2,0:T(8,128)(2,1)S(1)}, bf16[1,256,2048]{1,2,0:T(8,128)(2,1)S(1)}, u32[]{:S(2)}, u32[]{:S(2)}) collective-permute-start(bf16[1,256,2048]{1,2,0:T(8,128)(2,1)S(1)} %copy.7), channel_id=1, source_target_pairs={{8,0},{16,8},{24,16},{32,24},{40,32},{48,40},{56,48},{64,56},{72,6... | collective-permute-start | bytes 3145736 | tf_op jit(solution)/shard_map/ppermute | solution.py:18
  72.5 26.5 %collective-permute-start.2 = (bf16[1,256,2048]{1,2,0:T(8,128)(2,1)S(1)}, bf16[1,256,2048]{1,2,0:T(8,128)(2,1)}, u32[]{:S(2)}, u32[]{:S(2)}) collective-permute-start(bf16[1,256,2048]{1,2,0:T(8,128)(2,1)S(1)} %copy.7), channel_id=1, source_target_pairs={{0,8},{8,16},{16,24},{24,32},{32,40},{40,48},{48,56},{56,64},{64,7... | collective-permute-start | bytes 3145736 | tf_op jit(solution)/shard_map/ppermute | solution.py:15
  76.3 6.1 %copy-start.54 = (bf16[1,32,2048]{2,1,0:T(8,128)(2,1)S(1)}, bf16[1,32,2048]{2,1,0:T(8,128)(2,1)}, u32[]{:S(2)}) copy-start(bf16[1,32,2048]{2,1,0:T(8,128)(2,1)} %param.3) | copy-start | bytes 393220
  76.3 6.1 %copy-start.57 = (bf16[1,32,2048]{2,1,0:T(8,128)(2,1)S(1)}, bf16[1,32,2048]{2,1,0:T(8,128)(2,1)}, u32[]{:S(2)}) copy-start(bf16[1,32,2048]{2,1,0:T(8,128)(2,1)} %copy-done.55) | copy-start | bytes 393220
  76.3 6.0 %copy-start.60 = (bf16[1,32,2048]{2,1,0:T(8,128)(2,1)S(1)}, bf16[1,32,2048]{2,1,0:T(8,128)(2,1)}, u32[]{:S(2)}) copy-start(bf16[1,32,2048]{2,1,0:T(8,128)(2,1)} %copy-done.58) | copy-start | bytes 393220
  78.5 5.0 %copy-start.28 = (bf16[1,32,2048]{2,1,0:T(8,128)(2,1)S(1)}, bf16[1,32,2048]{2,1,0:T(8,128)(2,1)}, u32[]{:S(2)}) copy-start(bf16[1,32,2048]{2,1,0:T(8,128)(2,1)} %copy-done.27) | copy-start | bytes 393220
  78.5 5.0 %copy-start.32 = (bf16[1,32,2048]{2,1,0:T(8,128)(2,1)S(1)}, bf16[1,32,2048]{2,1,0:T(8,128)(2,1)}, u32[]{:S(2)}) copy-start(bf16[1,32,2048]{2,1,0:T(8,128)(2,1)} %copy-done.31) | copy-start | bytes 393220
  78.5 5.0 %copy-start.37 = (bf16[1,32,2048]{2,1,0:T(8,128)(2,1)S(1)}, bf16[1,32,2048]{2,1,0:T(8,128)(2,1)}, u32[]{:S(2)}) copy-start(bf16[1,32,2048]{2,1,0:T(8,128)(2,1)} %copy-done.36) | copy-start | bytes 393220
  80.6 4.0 %copy-start.30 = (bf16[1,32,2048]{2,1,0:T(8,128)(2,1)S(1)}, bf16[1,32,2048]{2,1,0:T(8,128)(2,1)}, u32[]{:S(2)}) copy-start(bf16[1,32,2048]{2,1,0:T(8,128)(2,1)} %copy-done.29) | copy-start | bytes 393220
  80.6 4.0 %copy-start.34 = (bf16[1,32,2048]{2,1,0:T(8,128)(2,1)S(1)}, bf16[1,32,2048]{2,1,0:T(8,128)(2,1)}, u32[]{:S(2)}) copy-start(bf16[1,32,2048]{2,1,0:T(8,128)(2,1)} %copy-done.33) | copy-start | bytes 393220
  80.6 4.0 %copy-start.39 = (bf16[1,32,2048]{2,1,0:T(8,128)(2,1)S(1)}, bf16[1,32,2048]{2,1,0:T(8,128)(2,1)}, u32[]{:S(2)}) copy-start(bf16[1,32,2048]{2,1,0:T(8,128)(2,1)} %copy-done.38) | copy-start | bytes 393220
  81.7 3.9 %copy-start.24 = (bf16[1,32,2048]{2,1,0:T(8,128)(2,1)S(1)}, bf16[1,32,2048]{2,1,0:T(8,128)(2,1)}, u32[]{:S(2)}) copy-start(bf16[1,32,2048]{2,1,0:T(8,128)(2,1)} %slice.787) | copy-start | bytes 393220
  81.8 3.9 %copy-start.26 = (bf16[1,32,2048]{2,1,0:T(8,128)(2,1)S(1)}, bf16[1,32,2048]{2,1,0:T(8,128)(2,1)}, u32[]{:S(2)}) copy-start(bf16[1,32,2048]{2,1,0:T(8,128)(2,1)} %copy-done.25) | copy-start | bytes 393220
  82.9 3.9 %copy-start.22 = (bf16[1,32,2048]{2,1,0:T(8,128)(2,1)S(1)}, bf16[1,32,2048]{2,1,0:T(8,128)(2,1)}, u32[]{:S(2)}) copy-start(bf16[1,32,2048]{2,1,0:T(8,128)(2,1)} %slice.792) | copy-start | bytes 393220
  99.0 2.0 copy-start.13
  104.5 8.9 %copy-start.108 = (bf16[256,32]{0,1:T(8,128)(2,1)S(1)}, bf16[256,32]{0,1:T(8,128)(2,1)}, u32[]{:S(2)}) copy-start(bf16[256,32]{0,1:T(8,128)(2,1)} %get-tuple-element.75) | copy-start | bytes 49156
  104.5 8.9 %copy-start.109 = (bf16[256,32]{0,1:T(8,128)(2,1)S(1)}, bf16[256,32]{0,1:T(8,128)(2,1)}, u32[]{:S(2)}) copy-start(bf16[256,32]{0,1:T(8,128)(2,1)} %get-tuple-element.76) | copy-start | bytes 49156
  104.5 8.9 %copy-start.110 = (bf16[256,32]{0,1:T(8,128)(2,1)S(1)}, bf16[256,32]{0,1:T(8,128)(2,1)}, u32[]{:S(2)}) copy-start(bf16[256,32]{0,1:T(8,128)(2,1)} %get-tuple-element.77) | copy-start | bytes 49156
  113.4 3.1 copy-start.6
  113.4 3.1 copy-start.7
  113.4 3.1 copy-start.8
  113.5 3.1 copy-start.100
  113.5 3.1 copy-start.101
  113.5 3.1 copy-start.102
  122.7 2.3 copy-start.90
  122.7 2.3 copy-start.91
  122.7 2.3 copy-start.92
  (54 other events, 66.2 us)
Sparse Core Ops, SparseCore 0:
  16.7 49.8 all-gather.1
  70.6 82.0 reduce-scatter.1
  156.0 220.1 all-reduce.3
where the time goes:
time: 386 us; the launch traced here: 385 us
  waiting for transfers between devices  247 us (64%)
  local copies, waits for them, and re-layouts  75.3 us (20%)
  matrix products  27.3 us (7%)
  starting transfers between devices  15.7 us (4%)
  between operations  15.1 us (4%)
  other arithmetic  4.51 us (1%)
    psum x1, waiting for transfers between devices, local(): weight_grad = lax.psum(local_terms, 'space')  222 us
    slice x28, local copies, waits for them, and re-layouts, stack_at(): moved[tap_depth:tap_depth + planes]  43.6 us
    unnamed x249, local copies, waits for them, and re-layouts  23.1 us
    reduce_scatter x1, waiting for transfers between devices, local(): lax.psum_scatter(partial_out, 'chan', scatter_dimension=1, tiled=True)  22.9 us
    dot_general x18, matrix products, convolve(): jnp.einsum('dcp,co->dop', stack_at(padded, tap_row, tap_col), tap_weights...  19.7 us
    ppermute x2, starting transfers between devices, extended(): lax.ppermute(lax.slice_in_dim(block, 0, width, axis=dim), axis, backward)  11.7 us
  transfers between devices with their start and end apart: 7, of which 4 were waited for; matrix products, arithmetic and copies ran while one was open for 26% of the time, Pallas kernels for 0%

commit v1 on v0

--- a/solution.py
+++ b/solution.py
@@ -84,7 +84,12 @@
     flipped = jnp.transpose(weights[::-1], (0, 2, 1))
     input_grad = convolve(cot_padded, flipped).astype(jnp.bfloat16)
     local_terms = weight_terms(padded, cot_whole, inputs.shape[1])
-    weight_grad = lax.psum(local_terms, "space")
+
+    def put_positions(array_in, axis_id):
+        heard = jnp.sum(jax.lax.all_gather(array_in, axis_name=axis_id), axis=0)
+        return heard
+
+    weight_grad = put_positions(local_terms, "space")
     return (output, input_grad, weight_grad)
 
 

time: 386 us -> 339 us (0.88)
  waiting for transfers between devices: 247 us -> 217 us
  local copies, waits for them, and re-layouts: 75.3 us -> 49.5 us
  other arithmetic: 4.51 us -> 14.4 us
    psum x1 -> x0, waiting for transfers between devices: 222 us -> none  [local(): weight_grad = lax.psum(local_terms, 'space')]
    all_gather x0 -> x1, waiting for transfers between devices: none -> 159 us  [put_positions(): heard = jnp.sum(jax.lax.all_gather(array_in, axis_name=axis_id), axis=0)]
    unnamed x249 -> x182, local copies, waits for them, and re-layouts: 23.1 us -> 5.64 us
    reduce_sum x0 -> x1, other arithmetic: none -> 11.4 us  [put_positions(): heard = jnp.sum(jax.lax.all_gather(array_in, axis_name=axis_id), axis=0)]
    reduce_scatter x1, waiting for transfers between devices: 22.9 us -> 34.1 us  [local(): lax.psum_scatter(partial_out, 'chan', scatter_dimension=1, tiled=True)]
    ppermute x2, waiting for transfers between devices: 0.01 us -> 10.3 us  [extended(): lax.ppermute(lax.slice_in_dim(block, 0, width, axis=dim), axis, backward)]
    ppermute x2, waiting for transfers between devices: 0.95 us -> 9.43 us  [extended(): lax.ppermute(lax.slice_in_dim(block, block.shape[dim] - width, None, axis...]
    slice x28, local copies, waits for them, and re-layouts: 43.6 us -> 39.4 us  [stack_at(): moved[tap_depth:tap_depth + planes]]
  transfers between devices with their start and end apart: 7 -> 7, of which waited for: 4 -> 6; matrix products, arithmetic and copies ran while one was open for 26% -> 22% of each run, Pallas kernels for 0% -> 0%
where the time goes in v1:
time: 339 us; the launch traced here: 336 us
  waiting for transfers between devices  217 us (64%)
  local copies, waits for them, and re-layouts  49.5 us (15%)
  matrix products  27.1 us (8%)
  between operations  15 us (4%)
  other arithmetic  14.4 us (4%)
  starting transfers between devices  13.8 us (4%)
    all_gather x1, waiting for transfers between devices, put_positions(): heard = jnp.sum(jax.lax.all_gather(array_in, axis_name=axis_id), axis=0)  159 us
    slice x28, local copies, waits for them, and re-layouts, stack_at(): moved[tap_depth:tap_depth + planes]  39.4 us
    reduce_scatter x1, waiting for transfers between devices, local(): lax.psum_scatter(partial_out, 'chan', scatter_dimension=1, tiled=True)  34.1 us
    dot_general x18, matrix products, convolve(): jnp.einsum('dcp,co->dop', stack_at(padded, tap_row, tap_col), tap_weights...  18.3 us
    reduce_sum x1, other arithmetic, put_positions(): heard = jnp.sum(jax.lax.all_gather(array_in, axis_name=axis_id), axis=0)  11.4 us
    ppermute x2, waiting for transfers between devices, extended(): lax.ppermute(lax.slice_in_dim(block, 0, width, axis=dim), axis, backward)  10.3 us
    ppermute x2, starting transfers between devices, extended(): lax.ppermute(lax.slice_in_dim(block, 0, width, axis=dim), axis, backward)  9.84 us
    ppermute x2, waiting for transfers between devices, extended(): lax.ppermute(lax.slice_in_dim(block, block.shape[dim] - width, None, axis...  9.43 us
  transfers between devices with their start and end apart: 7, of which 6 were waited for; matrix products, arithmetic and copies ran while one was open for 22% of the time, Pallas kernels for 0%

profile of v1, /device:TPU:24, one launch (start us, length us, event | category | flops | bytes accessed | tf_op | source)
XLA Modules:
  0.0 336.5 jit_solution(10008134416257139854)
XLA Ops:
  7.2 7.4 %collective-permute-start.1 = (bf16[1,32,2048]{2,1,0:T(8,128)(2,1)}, bf16[1,32,2048]{2,1,0:T(8,128)(2,1)S(1)}, u32[]{:S(2)}, u32[]{:S(2)}) collective-permute-start(bf16[1,32,2048]{2,1,0:T(8,128)(2,1)} %param.3), channel_id=1, source_target_pairs={{8,0},{16,8},{24,16},{32,24},{40,32},{48,40},{56,48},{64,56},{72,6... | collective-permute-start | bytes 393224 | tf_op jit(solution)/shard_map/ppermute | solution.py:18
  14.6 1.9 collective-permute-start
  16.6 1.6 slice_bitcast_fusion.56
  18.3 1.5 slice_bitcast_fusion.54
  19.8 3.4 %collective-permute-done = bf16[1,32,2048]{2,1,0:T(8,128)(2,1)S(1)} collective-permute-done((bf16[1,32,2048]{2,1,0:T(8,128)(2,1)}, bf16[1,32,2048]{2,1,0:T(8,128)(2,1)S(1)}, u32[]{:S(2)}, u32[]{:S(2)}) %collective-permute-start) | collective-permute-done | bytes 131104 | tf_op jit(solution)/shard_map/ppermute | solution.py:15
  23.2 0.6 copy-done.52
  23.9 0.9 pad_maximum_fusion.1
  24.8 0.8 reshape.279
  25.6 2.8 pad_slice_fusion.26
  28.4 1.5 pad_slice_fusion.25
  29.9 1.3 slice.769
  31.2 1.9 slice.767
  33.1 1.9 slice.765
  35.0 1.9 slice.730
  36.8 1.9 slice.728
  38.7 1.9 slice.726
  40.6 1.9 slice.739
  42.5 1.9 slice.737
  44.4 0.9 slice.735
  45.3 0.9 slice.748
  46.2 0.9 slice.746
  47.1 0.9 slice.744
  48.1 0.9 slice.757
  49.0 0.9 slice.755
  49.9 0.9 slice.753
  51.7 1.3 slice.787
  55.0 1.5 fusion.76
  58.1 0.5 convolution_add_fusion.4
  58.7 0.5 fusion.46
  59.4 0.5 convolution_add_fusion.2
  59.9 0.6 convolution_add_fusion.1
  60.7 1.8 fusion.45
  62.5 4.1 %all-gather.4.cloned.1.call-done = bf16[1,256,2048]{2,1,0:T(8,128)(2,1)} async-done(((bf16[1,32,2048]{2,1,0:T(8,128)(2,1)}), bf16[1,256,2048]{2,1,0:T(8,128)(2,1)}) %all-gather.4.cloned.1.call-update) | async-done | bytes 1048592 | tf_op jit(solution)/shard_map/all_gather | solution.py:81
  66.6 1.8 fusion.73
  68.4 1.9 fusion.71
  70.3 1.4 fusion.69
  71.8 1.5 fusion.67
  73.3 0.5 fusion.65
  73.8 0.5 fusion.63
  74.3 0.5 fusion.61
  74.8 0.5 fusion.59
  75.3 0.5 fusion.57
  76.1 0.9 copy-done.19
  77.0 0.5 copy.7
  77.5 2.4 collective-permute-start.3
  80.0 1.9 collective-permute-start.2
  82.0 10.3 %collective-permute-done.3 = bf16[1,256,2048]{1,2,0:T(8,128)(2,1)S(1)} collective-permute-done((bf16[1,256,2048]{1,2,0:T(8,128)(2,1)S(1)}, bf16[1,256,2048]{1,2,0:T(8,128)(2,1)S(1)}, u32[]{:S(2)}, u32[]{:S(2)}) %collective-permute-start.3) | collective-permute-done | bytes 1048608 | tf_op jit(solution)/shard_map/ppermute | solution.py:18
  92.3 6.0 %collective-permute-done.2 = bf16[1,256,2048]{1,2,0:T(8,128)(2,1)S(1)} collective-permute-done((bf16[1,256,2048]{1,2,0:T(8,128)(2,1)S(1)}, bf16[1,256,2048]{1,2,0:T(8,128)(2,1)S(1)}, u32[]{:S(2)}, u32[]{:S(2)}) %collective-permute-start.2) | collective-permute-done | bytes 1048608 | tf_op jit(solution)/shard_map/ppermute | solution.py:15
  98.7 0.7 copy-done.14
  99.3 8.9 %pad_slice_fusion.2 = (bf16[1,256,32,64]{1,3,2,0:T(8,128)(2,1)S(1)}, bf16[1,256,32,64]{1,3,2,0:T(8,128)(2,1)}, bf16[1,256,32,64]{1,3,2,0:T(8,128)(2,1)}, bf16[1,...) fusion(bf16[3,256,32,64]{1,3,2,0:T(8,128)(2,1)S(1)} %bitcast.399), kind=kLoop, calls=%fused_computation.94 | loop fusion | bytes 23068672 | tf_op jit(solution)/shard_map/slice | solution.py:35
  108.2 2.9 fusion.25
  111.2 1.8 pad_slice_fusion.1
  113.0 1.0 fusion
  114.9 1.0 fusion.54
  116.8 1.0 fusion.53
  117.8 1.0 fusion.52
  119.4 1.0 fusion.51
  120.4 1.0 fusion.49
  121.4 1.0 fusion.48
  122.4 1.7 fusion.56
  124.1 34.1 %reduce-scatter.2.cloned.1.call-done = f32[1,32,2048]{2,1,0:T(8,128)} async-done(((f32[1,256,2048]{2,1,0:T(8,128)}), f32[1,32,2048]{2,1,0:T(8,128)}) %reduce-scatter.2.cloned.1.call-update) | async-done | bytes 262160 | tf_op jit(solution)/shard_map/reduce_scatter | solution.py:78
  158.2 1.6 convert_element_type.38
  159.8 158.7 %all-gather.6.cloned.1.call-done = f32[864,32,256]{2,1,0:T(8,128)} async-done(((f32[27,32,256]{2,1,0:T(8,128)}), f32[864,32,256]{2,1,0:T(8,128)}) %all-gather.6.cloned.1.call-update) | async-done | bytes 28311568 | tf_op jit(solution)/shard_map/all_gather | solution.py:89
  318.5 11.4 %reduce_sum.9 = f32[27,32,256]{2,1,0:T(8,128)} reduce(f32[32,27,32,256]{3,2,1,0:T(8,128)} %bitcast.398, f32[]{:T(128)} %constant.4.clone.1), dimensions={0}, to_apply=%region_1.2 | reduce | flops 6856704 | bytes 29196292 | tf_op jit(solution)/shard_map/reduce_sum | solution.py:89
  (202 shorter events, 7.6 us)
Async XLA Ops:
  7.2 59.4 %all-gather.4.cloned.1.call-start = ((), (), s32[]{:S(2)}) async-start(), calls=%async_computation.2 | async-start | bytes 1179648 | tf_op jit(solution)/shard_map/all_gather | solution.py:81
  7.2 12.6 %collective-permute-start.1 = (bf16[1,32,2048]{2,1,0:T(8,128)(2,1)}, bf16[1,32,2048]{2,1,0:T(8,128)(2,1)S(1)}, u32[]{:S(2)}, u32[]{:S(2)}) collective-permute-start(bf16[1,32,2048]{2,1,0:T(8,128)(2,1)} %param.3), channel_id=1, source_target_pairs={{8,0},{16,8},{24,16},{32,24},{40,32},{48,40},{56,48},{64,56},{72,6... | collective-permute-start | bytes 393224 | tf_op jit(solution)/shard_map/ppermute | solution.py:18
  14.6 8.6 %collective-permute-start = (bf16[1,32,2048]{2,1,0:T(8,128)(2,1)}, bf16[1,32,2048]{2,1,0:T(8,128)(2,1)S(1)}, u32[]{:S(2)}, u32[]{:S(2)}) collective-permute-start(bf16[1,32,2048]{2,1,0:T(8,128)(2,1)} %param.3), channel_id=1, source_target_pairs={{0,8},{8,16},{16,24},{24,32},{32,40},{40,48},{48,56},{56,64},{64,7... | collective-permute-start | bytes 393224 | tf_op jit(solution)/shard_map/ppermute | solution.py:15
  16.6 141.6 %reduce-scatter.2.cloned.1.call-start = ((), (), s32[]{:S(2)}) async-start(), calls=%async_computation.1 | async-start | bytes 2359296 | tf_op jit(solution)/shard_map/reduce_scatter | solution.py:78
  19.8 3.4 %copy-start.49 = (bf16[1,32,2048]{2,1,0:T(8,128)(2,1)}, bf16[1,32,2048]{2,1,0:T(8,128)(2,1)S(1)}, u32[]{:S(2)}) copy-start(bf16[1,32,2048]{2,1,0:T(8,128)(2,1)S(1)} %collective-permute-done.1) | copy-start | bytes 393220
  29.9 14.5 %copy-start.10 = (bf16[1,32,32,64]{3,2,1,0:T(8,128)(2,1)S(1)}, bf16[1,32,32,64]{3,2,1,0:T(8,128)(2,1)}, u32[]{:S(2)}) copy-start(bf16[1,32,32,64]{3,2,1,0:T(8,128)(2,1)} %get-tuple-element.30) | copy-start | bytes 393220
  29.9 15.4 %copy-start.9 = (bf16[1,32,32,64]{3,2,1,0:T(8,128)(2,1)S(1)}, bf16[1,32,32,64]{3,2,1,0:T(8,128)(2,1)}, u32[]{:S(2)}) copy-start(bf16[1,32,32,64]{3,2,1,0:T(8,128)(2,1)} %get-tuple-element.35) | copy-start | bytes 393220
  40.6 13.3 %copy-start.16 = (bf16[1,32,32,64]{3,2,1,0:T(8,128)(2,1)S(1)}, bf16[1,32,32,64]{3,2,1,0:T(8,128)(2,1)}, u32[]{:S(2)}) copy-start(bf16[1,32,32,64]{3,2,1,0:T(8,128)(2,1)} %get-tuple-element.46) | copy-start | bytes 393220
  45.3 8.3 %copy-start.17 = (bf16[1,32,32,64]{3,2,1,0:T(8,128)(2,1)S(1)}, bf16[1,32,32,64]{3,2,1,0:T(8,128)(2,1)}, u32[]{:S(2)}) copy-start(bf16[1,32,32,64]{3,2,1,0:T(8,128)(2,1)} %get-tuple-element.49) | copy-start | bytes 393220
  46.2 6.7 %copy-start.18 = (bf16[1,32,32,64]{3,2,1,0:T(8,128)(2,1)S(1)}, bf16[1,32,32,64]{3,2,1,0:T(8,128)(2,1)}, u32[]{:S(2)}) copy-start(bf16[1,32,32,64]{3,2,1,0:T(8,128)(2,1)} %get-tuple-element.47) | copy-start | bytes 393220
  47.1 7.3 %copy-start.20 = (bf16[1,32,2048]{2,1,0:T(8,128)(2,1)S(1)}, bf16[1,32,2048]{2,1,0:T(8,128)(2,1)}, u32[]{:S(2)}) copy-start(bf16[1,32,2048]{2,1,0:T(8,128)(2,1)} %slice.767) | copy-start | bytes 393220
  47.1 7.3 %copy-start.21 = (bf16[1,32,2048]{2,1,0:T(8,128)(2,1)S(1)}, bf16[1,32,2048]{2,1,0:T(8,128)(2,1)}, u32[]{:S(2)}) copy-start(bf16[1,32,2048]{2,1,0:T(8,128)(2,1)} %slice.765) | copy-start | bytes 393220
  48.1 6.4 %copy-start.71 = (bf16[32,256]{1,0:T(8,128)(2,1)S(1)}, bf16[32,256]{1,0:T(8,128)(2,1)}, u32[]{:S(2)}) copy-start(bf16[32,256]{1,0:T(8,128)(2,1)} %get-tuple-element.86) | copy-start | bytes 49156
  48.1 6.4 %copy-start.72 = (bf16[32,256]{1,0:T(8,128)(2,1)S(1)}, bf16[32,256]{1,0:T(8,128)(2,1)}, u32[]{:S(2)}) copy-start(bf16[32,256]{1,0:T(8,128)(2,1)} %get-tuple-element.87) | copy-start | bytes 49156
  48.1 6.4 %copy-start.73 = (bf16[32,256]{1,0:T(8,128)(2,1)S(1)}, bf16[32,256]{1,0:T(8,128)(2,1)}, u32[]{:S(2)}) copy-start(bf16[32,256]{1,0:T(8,128)(2,1)} %get-tuple-element.88) | copy-start | bytes 49156
  50.9 4.1 %copy-start.30 = (bf16[1,32,2048]{2,1,0:T(8,128)(2,1)S(1)}, bf16[1,32,2048]{2,1,0:T(8,128)(2,1)}, u32[]{:S(2)}) copy-start(bf16[1,32,2048]{2,1,0:T(8,128)(2,1)} %slice.730) | copy-start | bytes 393220
  50.9 4.1 %copy-start.32 = (bf16[1,32,2048]{2,1,0:T(8,128)(2,1)S(1)}, bf16[1,32,2048]{2,1,0:T(8,128)(2,1)}, u32[]{:S(2)}) copy-start(bf16[1,32,2048]{2,1,0:T(8,128)(2,1)} %slice.728) | copy-start | bytes 393220
  51.7 7.5 %copy-start.22 = (bf16[1,32,2048]{2,1,0:T(8,128)(2,1)}, bf16[1,32,2048]{2,1,0:T(8,128)(2,1)S(1)}, u32[]{:S(2)}) copy-start(bf16[1,32,2048]{2,1,0:T(8,128)(2,1)S(1)} %slice.774) | copy-start | bytes 393220
  53.5 6.4 %copy-start.24 = (bf16[1,32,2048]{2,1,0:T(8,128)(2,1)}, bf16[1,32,2048]{2,1,0:T(8,128)(2,1)S(1)}, u32[]{:S(2)}) copy-start(bf16[1,32,2048]{2,1,0:T(8,128)(2,1)S(1)} %slice.783) | copy-start | bytes 393220
  53.5 3.0 copy-start.34
  53.5 3.0 copy-start.41
  53.5 3.0 copy-start.44
  53.6 3.0 copy-start.75
  53.6 3.0 copy-start.76
  53.6 3.0 copy-start.77
  54.1 6.4 %copy-start.26 = (bf16[1,32,2048]{2,1,0:T(8,128)(2,1)}, bf16[1,32,2048]{2,1,0:T(8,128)(2,1)S(1)}, u32[]{:S(2)}) copy-start(bf16[1,32,2048]{2,1,0:T(8,128)(2,1)S(1)} %slice.794) | copy-start | bytes 393220
  54.4 6.2 %copy-start.28 = (bf16[1,32,2048]{2,1,0:T(8,128)(2,1)}, bf16[1,32,2048]{2,1,0:T(8,128)(2,1)S(1)}, u32[]{:S(2)}) copy-start(bf16[1,32,2048]{2,1,0:T(8,128)(2,1)S(1)} %slice.792) | copy-start | bytes 393220
  54.9 2.1 copy-start.36
  55.0 2.1 copy-start.42
  55.0 2.1 copy-start.45
  55.0 2.1 copy-start.69
  55.0 2.1 copy-start.70
  55.0 2.1 copy-start.74
  57.6 1.0 copy-start.53
  57.6 1.0 copy-start.62
  60.6 6.0 %copy-start.31 = (bf16[1,32,2048]{2,1,0:T(8,128)(2,1)S(1)}, bf16[1,32,2048]{2,1,0:T(8,128)(2,1)}, u32[]{:S(2)}) copy-start(bf16[1,32,2048]{2,1,0:T(8,128)(2,1)} %slice.730) | copy-start | bytes 393220
  60.6 6.0 %copy-start.33 = (bf16[1,32,2048]{2,1,0:T(8,128)(2,1)S(1)}, bf16[1,32,2048]{2,1,0:T(8,128)(2,1)}, u32[]{:S(2)}) copy-start(bf16[1,32,2048]{2,1,0:T(8,128)(2,1)} %slice.728) | copy-start | bytes 393220
  60.6 5.9 %copy-start.40 = (bf16[1,32,2048]{2,1,0:T(8,128)(2,1)S(1)}, bf16[1,32,2048]{2,1,0:T(8,128)(2,1)}, u32[]{:S(2)}) copy-start(bf16[1,32,2048]{2,1,0:T(8,128)(2,1)} %slice.726) | copy-start | bytes 393220
  62.4 6.0 %copy-start.35 = (bf16[1,32,2048]{2,1,0:T(8,128)(2,1)S(1)}, bf16[1,32,2048]{2,1,0:T(8,128)(2,1)}, u32[]{:S(2)}) copy-start(bf16[1,32,2048]{2,1,0:T(8,128)(2,1)} %slice.739) | copy-start | bytes 393220
  62.4 7.9 %copy-start.37 = (bf16[1,32,2048]{2,1,0:T(8,128)(2,1)S(1)}, bf16[1,32,2048]{2,1,0:T(8,128)(2,1)}, u32[]{:S(2)}) copy-start(bf16[1,32,2048]{2,1,0:T(8,128)(2,1)} %slice.748) | copy-start | bytes 393220
  62.4 9.4 %copy-start.39 = (bf16[1,32,2048]{2,1,0:T(8,128)(2,1)S(1)}, bf16[1,32,2048]{2,1,0:T(8,128)(2,1)}, u32[]{:S(2)}) copy-start(bf16[1,32,2048]{2,1,0:T(8,128)(2,1)} %slice.757) | copy-start | bytes 393220
  62.5 256.1 %all-gather.6.cloned.1.call-start = ((), (), s32[]{:S(2)}) async-start(), calls=%async_computation.3 | async-start | bytes 29196288 | tf_op jit(solution)/shard_map/all_gather | solution.py:89
  66.6 3.8 %copy-start.11 = (bf16[1,256,2048]{2,1,0:T(8,128)(2,1)S(1)}, bf16[1,256,2048]{2,1,0:T(8,128)(2,1)}, u32[]{:S(2)}) copy-start(bf16[1,256,2048]{2,1,0:T(8,128)(2,1)} %all-gather.4.cloned.1.call-done) | copy-start | bytes 3145732
  68.4 4.9 %copy-start.48 = (bf16[1,32,2048]{2,1,0:T(8,128)(2,1)S(1)}, bf16[1,32,2048]{2,1,0:T(8,128)(2,1)}, u32[]{:S(2)}) copy-start(bf16[1,32,2048]{2,1,0:T(8,128)(2,1)} %param.3) | copy-start | bytes 393220
  68.4 4.9 %copy-start.51 = (bf16[1,32,2048]{2,1,0:T(8,128)(2,1)S(1)}, bf16[1,32,2048]{2,1,0:T(8,128)(2,1)}, u32[]{:S(2)}) copy-start(bf16[1,32,2048]{2,1,0:T(8,128)(2,1)} %copy-done.49) | copy-start | bytes 393220
  68.4 4.9 %copy-start.54 = (bf16[1,32,2048]{2,1,0:T(8,128)(2,1)S(1)}, bf16[1,32,2048]{2,1,0:T(8,128)(2,1)}, u32[]{:S(2)}) copy-start(bf16[1,32,2048]{2,1,0:T(8,128)(2,1)} %copy-done.52) | copy-start | bytes 393220
  71.8 2.5 copy-start.23
  73.3 1.5 copy-start.25
  73.8 1.5 copy-start.27
  73.8 1.5 copy-start.29
  75.3 6.6 %copy-start = (bf16[27,32,256]{2,1,0:T(8,128)(2,1)S(1)}, bf16[27,32,256]{2,1,0:T(8,128)(2,1)}, u32[]{:S(2)}) copy-start(bf16[27,32,256]{2,1,0:T(8,128)(2,1)} %param.4) | copy-start | bytes 1327108
  77.5 14.8 %collective-permute-start.3 = (bf16[1,256,2048]{1,2,0:T(8,128)(2,1)S(1)}, bf16[1,256,2048]{1,2,0:T(8,128)(2,1)S(1)}, u32[]{:S(2)}, u32[]{:S(2)}) collective-permute-start(bf16[1,256,2048]{1,2,0:T(8,128)(2,1)S(1)} %copy.7), channel_id=1, source_target_pairs={{8,0},{16,8},{24,16},{32,24},{40,32},{48,40},{56,48},{64,56},{72,6... | collective-permute-start | bytes 3145736 | tf_op jit(solution)/shard_map/ppermute | solution.py:18
  80.0 18.3 %collective-permute-start.2 = (bf16[1,256,2048]{1,2,0:T(8,128)(2,1)S(1)}, bf16[1,256,2048]{1,2,0:T(8,128)(2,1)S(1)}, u32[]{:S(2)}, u32[]{:S(2)}) collective-permute-start(bf16[1,256,2048]{1,2,0:T(8,128)(2,1)S(1)} %copy.7), channel_id=1, source_target_pairs={{0,8},{8,16},{16,24},{24,32},{32,40},{40,48},{48,56},{56,64},{64,7... | collective-permute-start | bytes 3145736 | tf_op jit(solution)/shard_map/ppermute | solution.py:15
  92.3 6.3 %copy-start.12 = (bf16[1,256,2048]{1,2,0:T(8,128)(2,1)}, bf16[1,256,2048]{1,2,0:T(8,128)(2,1)S(1)}, u32[]{:S(2)}) copy-start(bf16[1,256,2048]{1,2,0:T(8,128)(2,1)S(1)} %collective-permute-done.3) | copy-start | bytes 3145732
  111.1 1.9 copy-start.7
  111.2 1.8 copy-start.8
  113.0 1.2 copy-start.4
  113.0 1.5 copy-start.5
  113.0 1.8 copy-start.6
  114.9 1.2 copy-start.1
  114.9 1.6 copy-start.2
  114.9 1.9 copy-start.3
  117.8 1.3 copy-start.13
  117.8 1.6 copy-start.15
  (21 other events, 18.3 us)
Sparse Core Ops, SparseCore 0:
  16.7 49.8 all-gather.3
  70.6 87.5 reduce-scatter.1
  160.6 157.8 all-gather.5
